TPU v7x, 128 devices: a whole 4x4x4 slice. The times are simulated.
128 devices in a mesh: fsdp: 32 (over z, y, core), fac: 4 (over x).
Axes of the slice: x: 4, y: 4, z: 4, core: 2. Of those that a mesh axis runs over, the one named last changes fastest.
Arguments:
- activations: bfloat16 [32768, 3072], P('fsdp'), may hold values from -6 to 6
- out_grads: bfloat16 [32768, 3072], P('fsdp', 'fac'), may hold values from -12 to 12
- token_ids: int32 [32768], P('fsdp'), may hold values from 0 to 32767
- forget_mask: int32 [32768], P('fsdp'), may hold values 0 or 1
- importance: float32 [32768], replicated, may hold values from 0.3 to 3
- in_inverse: bfloat16 [3072, 3072], P('fsdp'), may hold values from -1 to 3, as said below
- out_inverse: bfloat16 [3072, 3072], P(None, 'fac'), may hold values from -1 to 3, as said below
Outputs:
- newton_step: float32 [3072, 3072], P('fsdp', 'fac')
- residual: float32 [3072, 3072], P('fsdp', 'fac')
Inputs may be any that keep to these rules, and one draw needn't show every extreme that they name: `in_inverse`: symmetric and positive definite. `out_inverse`: symmetric and positive definite.
All inputs are finite; a program needn't handle non-finite values. No bound on the sum of `forget_mask` on one device may be relied on, other than what follows from the above.
Results may differ from a plain program's by a relative error of at most 0.03.
Values may be sent and summed in bfloat16 or wider, within the bound.
No kernel may reach another device: no remote copies, remote signals or barrier semaphores. Data moves between devices by JAX's collectives and lax.ppermute only.
A program may use at most 64 MiB of HBM per device.

v0:
```python
import math
import jax
import jax.numpy as jnp
from jax import lax
from jax.sharding import PartitionSpec as P

ITERS = 2
damping = 0.3


def add_columns(matrix, piece):
    return jnp.dot(matrix, piece, preferred_element_type=jnp.float32)


def transposed_term(matrix, right):
    return lax.dot_general(
        matrix, right, (((0,), (0,)), ((), ())), preferred_element_type=jnp.float32
    )


FSDP = ("pairs", "core")


def ring_product(piece, right):
    n = lax.axis_size("fac")
    me = lax.axis_index("fac")
    width = piece.shape[1]

    def right_block(k):
        return lax.dynamic_slice_in_dim(right, k % n * width, width, axis=0)

    total = add_columns(piece, right_block(me))
    ahead = piece
    behind = piece
    for step in range(1, n // 2 + 1):
        ahead = lax.ppermute(ahead, "fac", [(j, (j + 1) % n) for j in range(n)])
        total = total + add_columns(ahead, right_block(me - step))
        if 2 * step < n:
            behind = lax.ppermute(behind, "fac", [(j, (j - 1) % n) for j in range(n)])
            total = total + add_columns(behind, right_block(me + step))
    return total


def scatter_sum(partial):
    pairs, cores = (lax.axis_size("pairs"), lax.axis_size("core"))
    blocks = partial.reshape(pairs, cores, partial.shape[0] // (pairs * cores), partial.shape[1])
    on_chip = lax.all_to_all(blocks, "core", 1, 1, tiled=False)
    chip_sum = jnp.sum(on_chip.astype(jnp.float32), axis=1).astype(jnp.bfloat16)
    received = lax.all_to_all(chip_sum, "pairs", 0, 0, tiled=False)
    return lax.optimization_barrier(jnp.sum(received.astype(jnp.float32), axis=0))


def global_sums(*partials):
    devices = lax.axis_size("pairs") * lax.axis_size("core") * lax.axis_size("fac")
    stacked = jnp.broadcast_to(jnp.stack(partials)[None, :], (devices, len(partials)))
    received = lax.all_to_all(stacked, FSDP + ("fac",), 0, 0, tiled=True)
    total = jnp.sum(received, axis=0)
    return tuple((total[i] for i in range(len(partials))))


def body(activations, out_grads, token_ids, forget_mask, importance, in_inverse, out_inverse):
    tok_rows, d_in = activations.shape
    total = tok_rows * lax.axis_size("pairs") * lax.axis_size("core")
    keep = 1.0 - forget_mask.astype(jnp.float32)
    weights = importance[token_ids] * keep / total
    forget_grads = out_grads * forget_mask.astype(jnp.bfloat16)[:, None]
    grad_scale = 1.0 / math.sqrt(total)
    gradient = scatter_sum(
        (transposed_term(activations, forget_grads) * grad_scale).astype(jnp.bfloat16)
    )

    def gather_rows(matrix):
        return lax.all_gather(matrix.astype(jnp.bfloat16), FSDP, axis=0, tiled=True)

    def precondition(gathered):
        mixed = add_columns(in_inverse, gathered)
        mixed_low = mixed.astype(jnp.bfloat16)
        return jnp.dot(
            lax.all_gather(mixed_low, "fac", axis=1, tiled=True),
            out_inverse,
            preferred_element_type=jnp.float32,
        )

    def inner_part(left, right):
        return jnp.sum(left * right)

    d_out_part = out_inverse.shape[1]
    in_cols = lax.all_gather(
        lax.dynamic_slice_in_dim(
            in_inverse, lax.axis_index("fac") * d_out_part, d_out_part, axis=1
        ),
        FSDP,
        axis=0,
        tiled=True,
    )
    gradient, in_cols = lax.optimization_barrier((gradient, in_cols))
    residual = -gradient
    residual_rows = gather_rows(residual)
    gram_cols = d_in // lax.axis_size("fac")
    own_cols = lax.dynamic_slice_in_dim(
        activations, lax.axis_index("fac") * gram_cols, gram_cols, axis=1
    )
    weighted = (own_cols * weights[:, None]).astype(jnp.bfloat16)
    half = gram_cols // 2
    gram_first = transposed_term(activations, weighted[:, :half]).astype(jnp.bfloat16)
    gram_second = transposed_term(activations, weighted[:, half:]).astype(jnp.bfloat16)
    residual_rows, first_rows = lax.optimization_barrier((residual_rows, scatter_sum(gram_first)))
    precond = precondition(residual_rows)
    gram_own = jnp.concatenate([first_rows, scatter_sum(gram_second)], axis=1)
    gram_rows = lax.all_gather(gram_own.astype(jnp.bfloat16), "fac", axis=1, tiled=True)

    def curvature(matrix):
        return add_columns(gram_rows, gather_rows(matrix)) + damping * matrix

    direction = precond
    image = curvature(direction)
    image_rows = gather_rows(image)
    inner_now, energy = global_sums(inner_part(residual, precond), inner_part(direction, image))
    gram_inverse = lax.all_gather(
        add_columns(gram_rows, in_cols).astype(jnp.bfloat16), "fac", axis=1, tiled=True
    )
    alpha = inner_now / energy
    newton_step = alpha * direction
    residual = residual - alpha * image
    next_rows = (residual_rows.astype(jnp.float32) - alpha * image_rows.astype(jnp.float32)).astype(
        jnp.bfloat16
    )
    rows = in_inverse.shape[0]
    left = jnp.concatenate([in_inverse, gram_inverse], axis=0)
    both = add_columns(left, next_rows).astype(jnp.bfloat16)
    both_out = ring_product(both, out_inverse)
    precond = both_out[:rows]
    precond_image = both_out[rows:] + damping * precond
    inner_next, z_hz, z_hd, d_hz = global_sums(
        inner_part(residual, precond),
        inner_part(precond, precond_image),
        inner_part(precond, image),
        inner_part(direction, precond_image),
    )
    beta = inner_next / inner_now
    direction = precond + beta * direction
    image = precond_image + beta * image
    energy = z_hz + beta * (z_hd + d_hz) + beta * beta * energy
    alpha = inner_next / energy
    newton_step = newton_step + alpha * direction
    residual = residual - alpha * image
    return (newton_step, residual)


def solution(mesh):
    cores = 2
    split = jax.sharding.Mesh(
        mesh.devices.reshape(mesh.shape["fsdp"] // cores, cores, mesh.shape["fac"]),
        ("pairs", "core", "fac"),
    )
    placed = (P(FSDP, None), P(FSDP, "fac"), P(FSDP), P(FSDP), P(), P(FSDP, None), P(None, "fac"))
    return jax.shard_map(
        body,
        mesh=split,
        in_specs=placed,
        out_specs=(P(FSDP, "fac"), P(FSDP, "fac")),
        check_vma=False,
    )
```

profile of v0, /device:TPU:1, one launch (start us, length us, event | category | flops | bytes accessed | tf_op | source)
XLA Modules:
  0.0 333.9 jit_solution(15328082240654221681)
XLA Ops:
  9.6 9.4 %fusion.2 = bf16[3072,768]{0,1:T(8,128)(2,1)} fusion(bf16[1024,3072]{1,0:T(8,128)(2,1)} %param.7, bf16[1024,768]{1,0:T(8,128)(2,1)} %param.8, bf16[1024]{0:T(1024)(128)(2,1)S(1)} %convert_element_type.76), kind=kOutput, calls=%fused_computation.6 | convolution fusion | flops 4837343232 | bytes 12584960 | tf_op jit(solution)/shard_map/dot_general | solution.py:16
  19.0 6.7 %copy.24 = bf16[3072,768]{1,0:T(8,128)(2,1)} copy(bf16[3072,768]{0,1:T(8,128)(2,1)} %fusion.2) | data formatting | bytes 9437184 | tf_op jit(solution)/shard_map/convert_element_type | solution.py:69
  28.3 9.7 %all_to_all.42 = bf16[16,2,96,768]{3,2,0,1:T(8,128)(2,1)} all-to-all(bf16[16,2,96,768]{3,2,0,1:T(8,128)(2,1)S(1)} %copy.25), channel_id=1, replica_groups=mesh['pairs'=16,'core'=2,'fac'=4] {'core'}, dimensions={1} | all-to-all | bytes 9437184 | tf_op jit(solution)/shard_map/all_to_all | solution.py:47
  38.0 3.5 %reduce_sum.135 = bf16[16,96,768]{2,1,0:T(8,128)(2,1)S(1)} reduce(bf16[16,2,96,768]{3,2,0,1:T(8,128)(2,1)} %all_to_all.42, bf16[]{:T(256)} %constant.44.clone.1), dimensions={1}, to_apply=%region_0.0 | reduce | flops 1179648 | bytes 7077890 | tf_op jit(solution)/shard_map/reduce_sum | solution.py:48
  41.5 43.2 %all_to_all.43 = bf16[16,96,768]{2,1,0:T(8,128)(2,1)S(1)} all-to-all(bf16[16,96,768]{2,1,0:T(8,128)(2,1)S(1)} %reduce_sum.135), channel_id=1, replica_groups=mesh['pairs'=16,'core'=2,'fac'=4] {'pairs'}, dimensions={0} | all-to-all | bytes 4718592 | tf_op jit(solution)/shard_map/all_to_all | solution.py:49
  85.9 6.2 %gather_fusion = f32[1024]{0:T(1024)S(1)} fusion(f32[32768]{0:T(1024)S(1)} %copy-done, s32[1024]{0:T(1024)S(1)} %fusion.19), kind=kCustom, calls=%fused_computation | custom fusion | bytes 12288 | tf_op jit(solution)/shard_map/gather | solution.py:65
  95.0 7.0 %fusion.3 = bf16[3072,384]{0,1:T(8,128)(2,1)} fusion(bf16[1024,3072]{1,0:T(8,128)(2,1)} %param.7, bf16[1024,768]{1,0:T(8,128)(2,1)S(1)} %multiply_convert_fusion.1), kind=kOutput, calls=%fused_computation.9 | convolution fusion | flops 2417098752 | bytes 9437184 | tf_op jit(solution)/shard_map/dot_general | solution.py:16
  105.2 6.1 %all_to_all.44 = bf16[16,2,96,384]{3,2,0,1:T(8,128)(2,1)S(1)} all-to-all(bf16[16,2,96,384]{3,2,0,1:T(8,128)(2,1)S(1)} %copy.27), channel_id=1, replica_groups=mesh['pairs'=16,'core'=2,'fac'=4] {'core'}, dimensions={1} | all-to-all | bytes 4718592 | tf_op jit(solution)/shard_map/all_to_all | solution.py:47
  113.1 30.0 %all_to_all.45 = bf16[16,96,384]{2,1,0:T(8,128)(2,1)S(1)} all-to-all(bf16[16,96,384]{2,1,0:T(8,128)(2,1)} %reduce_sum.137), channel_id=1, replica_groups=mesh['pairs'=16,'core'=2,'fac'=4] {'pairs'}, dimensions={0} | all-to-all | bytes 2359296 | tf_op jit(solution)/shard_map/all_to_all | solution.py:49
  148.5 11.5 %all_gather.23 = bf16[96,3072]{1,0:T(8,128)(2,1)S(1)} all-gather(bf16[96,768]{1,0:T(8,128)(2,1)S(1)} %fusion.15), channel_id=1, replica_groups=mesh['pairs'=16,'core'=2,'fac'=4] {'fac'}, dimensions={1}, use_global_device_ids=true | all-gather | bytes 737280 | tf_op jit(solution)/shard_map/all_gather | solution.py:79
  160.0 3.9 %fusion.27 = (bf16[96,768]{1,0:T(8,128)(2,1)}, f32[96,768]{1,0:T(8,128)S(1)}) fusion(bf16[96,3072]{1,0:T(8,128)(2,1)S(1)} %all_gather.23, bf16[3072,768]{1,0:T(8,128)(2,1)} %param.13), kind=kOutput, calls=%fused_computation.59 | convolution fusion | flops 453058560 | bytes 5750784 | tf_op jit(solution)/shard_map/dot_general | solution.py:78
  163.9 6.8 %fusion.4 = bf16[3072,384]{0,1:T(8,128)(2,1)} fusion(bf16[1024,3072]{1,0:T(8,128)(2,1)} %param.7, bf16[1024,768]{1,0:T(8,128)(2,1)S(1)} %copy-done.3), kind=kOutput, calls=%fused_computation.10 | convolution fusion | flops 2417098752 | bytes 9437184 | tf_op jit(solution)/shard_map/dot_general | solution.py:16
  174.0 7.5 %all_to_all.46 = bf16[16,2,96,384]{3,2,0,1:T(8,128)(2,1)S(1)} all-to-all(bf16[16,2,96,384]{3,2,0,1:T(8,128)(2,1)S(1)} %copy.29), channel_id=1, replica_groups=mesh['pairs'=16,'core'=2,'fac'=4] {'core'}, dimensions={1} | all-to-all | bytes 4718592 | tf_op jit(solution)/shard_map/all_to_all | solution.py:47
  183.3 26.3 %all_to_all.47 = bf16[16,96,384]{2,1,0:T(8,128)(2,1)S(1)} all-to-all(bf16[16,96,384]{2,1,0:T(8,128)(2,1)} %reduce_sum.140), channel_id=1, replica_groups=mesh['pairs'=16,'core'=2,'fac'=4] {'pairs'}, dimensions={0} | all-to-all | bytes 2359296 | tf_op jit(solution)/shard_map/all_to_all | solution.py:49
  209.8 11.7 %all_gather.24 = bf16[96,3072]{1,0:T(8,128)(2,1)S(1)} all-gather(bf16[96,768]{1,0:T(8,128)(2,1)S(1)} %pad_maximum_fusion), channel_id=1, replica_groups=mesh['pairs'=16,'core'=2,'fac'=4] {'fac'}, dimensions={1}, use_global_device_ids=true | all-gather | bytes 737280 | tf_op jit(solution)/shard_map/all_gather | solution.py:110
  221.5 4.5 %multiply_reduce_fusion.5 = (f32[]{:T(128)}, f32[]{:T(128)}, bf16[96,768]{1,0:T(8,128)(2,1)}, f32[96,768]{1,0:T(8,128)S(1)}) fusion(f32[96,768]{1,0:T(8,128)S(1)} %get-tuple-element.26, f32[96,768]{1,0:T(8,128)S(1)} %convert_reduce_fusion, bf16[96,3072]{1,0:T(8,128)(2,1)S(1)} %all_gather.24, bf16[3072,768]{1,0:T(8,128)(2,1)} %all-gather.9.cloned.1.call-done), kind=kOutput, calls=%fused_computation.43 | convolution fusion | flops 453574656 | bytes 6340616 | tf_op jit(solution)/shard_map/dot_general | solution.py:12
  226.0 3.3 convolution_convert_fusion.3
  231.3 10.9 %all-to-all-start.6 = ((f32[128,1,2]{2,1,0:T(1,128)}), f32[128,1,2]{2,1,0:T(1,128)S(1)}, u32[]{:S(2)}, u32[]{:S(2)}) async-start(f32[128,1,2]{2,1,0:T(1,128)} %broadcast_in_dim.7), calls=%async_computation.6 | async-start | bytes 131072 | tf_op jit(solution)/shard_map/all_to_all | solution.py:56
  242.2 11.3 %all_gather.26 = bf16[96,3072]{1,0:T(8,128)(2,1)S(1)} all-gather(bf16[96,768]{1,0:T(8,128)(2,1)S(1)} %convolution_convert_fusion.3), channel_id=1, replica_groups=mesh['pairs'=16,'core'=2,'fac'=4] {'fac'}, dimensions={1}, use_global_device_ids=true | all-gather | bytes 737280 | tf_op jit(solution)/shard_map/all_gather | solution.py:119
  255.7 20.6 %all-gather.11.cloned.1.call-done = bf16[3072,768]{1,0:T(8,128)(2,1)} async-done(((bf16[96,768]{1,0:T(8,128)(2,1)}), bf16[3072,768]{1,0:T(8,128)(2,1)}) %all-gather.11.cloned.1.call-update) | async-done | bytes 4718608 | tf_op jit(solution)/shard_map/all_gather | solution.py:73
  276.2 5.6 %fusion.6 = bf16[192,768]{1,0:T(8,128)(2,1)S(1)} fusion(bf16[3072,768]{1,0:T(8,128)(2,1)} %all-gather.11.cloned.1.call-done, bf16[3072,768]{1,0:T(8,128)(2,1)} %all-gather.7.cloned.1.call-done, f32[]{:T(128)S(6)} %div.17, bf16[96,3072]{1,0:T(8,128)(2,1)S(1)} %all_gather.26, bf16[96,3072]{1,0:T(8,128)(2,1)S(1)} %copy-done.5), kind=kOutput, calls=%fused_computation.18 | convolution fusion | flops 920272896 | bytes 10911748 | tf_op jit(solution)/shard_map/dot_general | solution.py:12
  286.2 5.2 %collective-permute-done = bf16[192,768]{1,0:T(8,128)(2,1)S(1)} collective-permute-done((bf16[192,768]{1,0:T(8,128)(2,1)S(1)}, bf16[192,768]{1,0:T(8,128)(2,1)S(1)}, u32[]{:S(2)}, u32[]{:S(2)}) %collective-permute-start) | collective-permute-done | bytes 294944 | tf_op jit(solution)/shard_map/ppermute | solution.py:36
  294.9 5.2 %collective-permute-done.2 = bf16[192,768]{1,0:T(8,128)(2,1)S(1)} collective-permute-done((bf16[192,768]{1,0:T(8,128)(2,1)S(1)}, bf16[192,768]{1,0:T(8,128)(2,1)S(1)}, u32[]{:S(2)}, u32[]{:S(2)}) %collective-permute-start.2) | collective-permute-done | bytes 294944 | tf_op jit(solution)/shard_map/ppermute | solution.py:36
  305.2 16.0 %all_to_all.48 = f32[128,1,4]{2,1,0:T(1,128)S(1)} all-to-all(f32[128,1,4]{2,1,0:T(1,128)S(1)} %broadcast_in_dim.8), channel_id=1, replica_groups=mesh['pairs'=16,'core'=2,'fac'=4] {'pairs','core','fac'}, dimensions={0} | all-to-all | bytes 4096 | tf_op jit(solution)/shard_map/all_to_all | solution.py:56
  (64 shorter events, 42.1 us)
Async XLA Ops:
  7.2 78.7 %copy-start = (f32[32768]{0:T(1024)S(1)}, f32[32768]{0:T(1024)}, u32[]{:S(2)}) copy-start(f32[32768]{0:T(1024)} %param.11) | copy-start | bytes 393220
  7.2 77.9 %all-gather.5.cloned.1.call-start = ((), (), s32[]{:S(2)}) async-start(), calls=%async_computation.8 | async-start | bytes 4866048 | tf_op jit(solution)/shard_map/all_gather | solution.py:88
  8.8 136.4 %all-gather.7.cloned.1.call-start = ((), (), s32[]{:S(2)}) async-start(), calls=%async_computation.9 | async-start | bytes 4866048 | tf_op jit(solution)/shard_map/all_gather | solution.py:73
  41.5 44.3 %copy-start.7 = (s32[1024]{0:T(1024)S(1)}, s32[1024]{0:T(1024)}, u32[]{:S(2)}) copy-start(s32[1024]{0:T(1024)} %param.9) | copy-start | bytes 12292
  84.7 7.3 %copy-start.6 = (s32[1024]{0:T(1024)S(1)}, s32[1024]{0:T(1024)}, u32[]{:S(2)}) copy-start(s32[1024]{0:T(1024)} %param.10) | copy-start | bytes 12292
  85.8 135.7 %all-gather.9.cloned.1.call-start = ((), (), s32[]{:S(2)}) async-start(), calls=%async_computation.10 | async-start | bytes 4866048 | tf_op jit(solution)/shard_map/all_gather | solution.py:73
  93.8 1.1 copy-start.2
  111.3 34.0 %copy-start.4 = (bf16[96,3072]{1,0:T(8,128)(2,1)S(1)}, bf16[96,3072]{1,0:T(8,128)(2,1)}, u32[]{:S(2)}) copy-start(bf16[96,3072]{1,0:T(8,128)(2,1)} %param.12) | copy-start | bytes 1769476
  143.2 20.7 %copy-start.3 = (bf16[1024,768]{1,0:T(8,128)(2,1)S(1)}, bf16[1024,768]{1,0:T(8,128)(2,1)}, u32[]{:S(2)}) copy-start(bf16[1024,768]{1,0:T(8,128)(2,1)} %copy-done.2) | copy-start | bytes 4718596
  163.9 112.4 %all-gather.11.cloned.1.call-start = ((), (), s32[]{:S(2)}) async-start(), calls=%async_computation.11 | async-start | bytes 4866048 | tf_op jit(solution)/shard_map/all_gather | solution.py:73
  226.0 50.3 %copy-start.5 = (bf16[96,3072]{1,0:T(8,128)(2,1)S(1)}, bf16[96,3072]{1,0:T(8,128)(2,1)}, u32[]{:S(2)}) copy-start(bf16[96,3072]{1,0:T(8,128)(2,1)} %param.12) | copy-start | bytes 1769476
  231.3 22.2 %all-to-all-start.6 = ((f32[128,1,2]{2,1,0:T(1,128)}), f32[128,1,2]{2,1,0:T(1,128)S(1)}, u32[]{:S(2)}, u32[]{:S(2)}) async-start(f32[128,1,2]{2,1,0:T(1,128)} %broadcast_in_dim.7), calls=%async_computation.6 | async-start | bytes 131072 | tf_op jit(solution)/shard_map/all_to_all | solution.py:56
  281.8 9.6 %collective-permute-start = (bf16[192,768]{1,0:T(8,128)(2,1)S(1)}, bf16[192,768]{1,0:T(8,128)(2,1)S(1)}, u32[]{:S(2)}, u32[]{:S(2)}) collective-permute-start(bf16[192,768]{1,0:T(8,128)(2,1)S(1)} %fusion.6), channel_id=1, source_target_pairs={{0,1},{1,2},{2,3},{3,0},{4,5},{5,6},{6,7},{7,4},{8,9},{9,10},{10,1... | collective-permute-start | bytes 884744 | tf_op jit(solution)/shard_map/ppermute | solution.py:36
  283.1 10.1 %collective-permute-start.1 = (bf16[192,768]{1,0:T(8,128)(2,1)S(1)}, bf16[192,768]{1,0:T(8,128)(2,1)S(1)}, u32[]{:S(2)}, u32[]{:S(2)}) collective-permute-start(bf16[192,768]{1,0:T(8,128)(2,1)S(1)} %fusion.6), channel_id=1, source_target_pairs={{0,3},{1,0},{2,1},{3,2},{4,7},{5,4},{6,5},{7,6},{8,11},{9,8},{10,9... | collective-permute-start | bytes 884744 | tf_op jit(solution)/shard_map/ppermute | solution.py:39
  291.4 8.6 %collective-permute-start.2 = (bf16[192,768]{1,0:T(8,128)(2,1)S(1)}, bf16[192,768]{1,0:T(8,128)(2,1)S(1)}, u32[]{:S(2)}, u32[]{:S(2)}) collective-permute-start(bf16[192,768]{1,0:T(8,128)(2,1)S(1)} %collective-permute-done), channel_id=1, source_target_pairs={{0,1},{1,2},{2,3},{3,0},{4,5},{5,6},{6,7},{7,4},{8,9},{9,10},{10,1... | collective-permute-start | bytes 884744 | tf_op jit(solution)/shard_map/ppermute | solution.py:36
  291.4 35.9 %copy-start.1 = (f32[32768]{0:T(1024)S(1)}, f32[32768]{0:T(1024)}, u32[]{:S(2)}) copy-start(f32[32768]{0:T(1024)} %param.11) | copy-start | bytes 393220
Sparse Core Ops, SparseCore 0:
  10.8 68.8 all-gather.4
  85.9 59.2 all-gather.6
  164.0 53.3 all-gather.8
  226.1 50.0 all-gather.10
where the time goes:
time: 335 us; the launch traced here: 334 us
  blocking collectives  173 us (52%)
  matrix products  50.4 us (15%)
  waiting for transfers between devices  33.1 us (10%)
  local copies, waits for them, and re-layouts  26.6 us (8%)
  between operations  19.9 us (6%)
  other arithmetic  16.8 us (5%)
  starting transfers between devices  13.8 us (4%)
    all_to_all x3, blocking collectives, scatter_sum(): received = lax.all_to_all(chip_sum, 'pairs', 0, 0, tiled=False)  99.5 us
    all_to_all x3, blocking collectives, scatter_sum(): on_chip = lax.all_to_all(blocks, 'core', 1, 1, tiled=False)  23.4 us
    dot_general x8, matrix products, add_columns(): return jnp.dot(matrix, piece, preferred_element_type=jnp.float32)  23.3 us
    dot_general x3, matrix products, transposed_term(): lax.dot_general(matrix, right, (((0,), (0,)), ((), ())), preferred_elemen...  23.2 us
    all_gather x3, waiting for transfers between devices, gather_rows(): return lax.all_gather(matrix.astype(jnp.bfloat16), FSDP, axis=0, tiled=True)  22.6 us
    all_to_all x1, blocking collectives, global_sums(): received = lax.all_to_all(stacked, FSDP + ('fac',), 0, 0, tiled=True)  16 us
    all_gather x1, blocking collectives, body(): lax.all_gather(gram_own.astype(jnp.bfloat16), 'fac', axis=1, tiled=True)  11.7 us
    all_gather x1, blocking collectives, precondition(): lax.all_gather(mixed_low, 'fac', axis=1, tiled=True)  11.5 us
  transfers between devices with their start and end apart: 8, of which 4 were waited for; matrix products, arithmetic and copies ran while one was open for 20% of the time, Pallas kernels for 0%

commit v1 on v0

--- a/solution.py
+++ b/solution.py
@@ -6,6 +6,9 @@
 
 ITERS = 2
 damping = 0.3
+fix_views = lambda local, which_dim: jnp.concatenate(
+    lax.all_to_all(jnp.stack(lax.axis_size(FSDP) * [local], axis=0), FSDP, 0, 0), axis=which_dim
+)
 
 
 def add_columns(matrix, piece):
@@ -70,7 +73,7 @@
     )
 
     def gather_rows(matrix):
-        return lax.all_gather(matrix.astype(jnp.bfloat16), FSDP, axis=0, tiled=True)
+        return fix_views(matrix.astype(jnp.bfloat16), 0)
 
     def precondition(gathered):
         mixed = add_columns(in_inverse, gathered)

time: 335 us -> 472 us (1.41)
  waiting for transfers between devices: 33.1 us -> 191 us
  blocking collectives: 173 us -> 81.3 us
  starting transfers between devices: 13.8 us -> 56.6 us
  other arithmetic: 16.8 us -> 33.4 us
  local copies, waits for them, and re-layouts: 26.6 us -> 39.8 us
    all_to_all x1 -> x8, waiting for transfers between devices: 0.01 us -> 184 us  [the longest x3 137 us: lax.all_to_all(jnp.stack(lax.axis_size(FSDP) * [local], axis=0), FSDP, 0, 0)]
    all_to_all x3 -> x0, blocking collectives: 99.5 us -> none  [scatter_sum(): received = lax.all_to_all(chip_sum, 'pairs', 0, 0, tiled=False)]
    all_to_all x1 -> x8, starting transfers between devices: 10.9 us -> 53.8 us  [the longest x3 24.5 us: lax.all_to_all(jnp.stack(lax.axis_size(FSDP) * [local], axis=0), FSDP, 0, 0)]
    all_gather x3 -> x0, waiting for transfers between devices: 22.6 us -> none  [gather_rows(): return lax.all_gather(matrix.astype(jnp.bfloat16), FSDP, axis=0, tiled=True)]
    all_to_all x1 -> x2, blocking collectives: 16 us -> 37.6 us  [global_sums(): received = lax.all_to_all(stacked, FSDP + ('fac',), 0, 0, tiled=True)]
    all_to_all x3 -> x1, blocking collectives: 23.4 us -> 8.87 us  [scatter_sum(): on_chip = lax.all_to_all(blocks, 'core', 1, 1, tiled=False)]
    another operation x0 -> x3, local copies, waits for them, and re-layouts: none -> 8.1 us  [jnp.stack(lax.axis_size(FSDP) * [local], axis=0)]
    convert_element_type x1 -> x2, other arithmetic: 0.68 us -> 7.03 us  [the longest x1 7.01 us: body(): (residual_rows.astype(jnp.float32) - alpha * image_rows.astype(jnp.float3...]
  transfers between devices with their start and end apart: 8 -> 12, of which waited for: 4 -> 7; matrix products, arithmetic and copies ran while one was open for 20% -> 18% of each run, Pallas kernels for 0% -> 0%
where the time goes in v1:
time: 472 us; the launch traced here: 470 us
  waiting for transfers between devices  191 us (40%)
  blocking collectives  81.3 us (17%)
  starting transfers between devices  56.6 us (12%)
  matrix products  47.9 us (10%)
  local copies, waits for them, and re-layouts  39.8 us (8%)
  other arithmetic  33.4 us (7%)
  between operations  20.1 us (4%)
    all_to_all x3, waiting for transfers between devices, lax.all_to_all(jnp.stack(lax.axis_size(FSDP) * [local], axis=0), FSDP, 0, 0)  137 us
    all_to_all x3, waiting for transfers between devices, scatter_sum(): received = lax.all_to_all(chip_sum, 'pairs', 0, 0, tiled=False)  47.5 us
    all_to_all x2, blocking collectives, global_sums(): received = lax.all_to_all(stacked, FSDP + ('fac',), 0, 0, tiled=True)  37.6 us
    all_to_all x3, starting transfers between devices, lax.all_to_all(jnp.stack(lax.axis_size(FSDP) * [local], axis=0), FSDP, 0, 0)  24.5 us
    dot_general x3, matrix products, transposed_term(): lax.dot_general(matrix, right, (((0,), (0,)), ((), ())), preferred_elemen...  23.1 us
    dot_general x8, matrix products, add_columns(): return jnp.dot(matrix, piece, preferred_element_type=jnp.float32)  21.6 us
    all_to_all x3, starting transfers between devices, scatter_sum(): received = lax.all_to_all(chip_sum, 'pairs', 0, 0, tiled=False)  17.9 us
    all_gather x1, blocking collectives, body(): lax.all_gather(add_columns(gram_rows, in_cols).astype(jnp.bfloat16), 'fac...  11.9 us
  transfers between devices with their start and end apart: 12, of which 7 were waited for; matrix products, arithmetic and copies ran while one was open for 18% of the time, Pallas kernels for 0%

profile of v1, /device:TPU:1, one launch (start us, length us, event | category | flops | bytes accessed | tf_op | source)
XLA Modules:
  0.0 470.5 jit_solution(18277999471938959987)
XLA Ops:
  9.5 9.3 %fusion.1 = bf16[3072,768]{0,1:T(8,128)(2,1)} fusion(bf16[1024,3072]{1,0:T(8,128)(2,1)} %param.7, bf16[1024,768]{1,0:T(8,128)(2,1)} %param.8, bf16[1024]{0:T(1024)(128)(2,1)S(1)} %convert_element_type.77), kind=kOutput, calls=%fused_computation.6 | convolution fusion | flops 4837343232 | bytes 12584960 | tf_op jit(solution)/shard_map/dot_general | solution.py:19
  18.9 6.7 %copy.24 = bf16[3072,768]{1,0:T(8,128)(2,1)} copy(bf16[3072,768]{0,1:T(8,128)(2,1)} %fusion.1) | data formatting | bytes 9437184 | tf_op jit(solution)/shard_map/convert_element_type | solution.py:72
  30.5 7.4 %all-to-all-start = ((bf16[16,2,96,768]{3,2,0,1:T(8,128)(2,1)}), bf16[16,2,96,768]{3,2,0,1:T(8,128)(2,1)}, u32[]{:S(2)}, u32[]{:S(2)}) async-start(bf16[16,2,96,768]{3,2,0,1:T(8,128)(2,1)} %copy.25), calls=%async_computation | async-start | bytes 9437184 | tf_op jit(solution)/shard_map/all_to_all | solution.py:50
  37.9 6.2 %gather_fusion = f32[1024]{0:T(1024)S(1)} fusion(f32[32768]{0:T(1024)S(1)} %copy-done, s32[1024]{0:T(1024)S(1)} %fusion.17), kind=kCustom, calls=%fused_computation | custom fusion | bytes 12288 | tf_op jit(solution)/shard_map/gather | solution.py:68
  47.0 6.9 %fusion.3 = bf16[3072,384]{0,1:T(8,128)(2,1)} fusion(bf16[1024,3072]{1,0:T(8,128)(2,1)} %param.7, bf16[1024,768]{1,0:T(8,128)(2,1)S(1)} %multiply_convert_fusion.1), kind=kOutput, calls=%fused_computation.10 | convolution fusion | flops 2417098752 | bytes 9437184 | tf_op jit(solution)/shard_map/dot_general | solution.py:19
  59.1 6.9 %fusion.2 = bf16[3072,384]{0,1:T(8,128)(2,1)} fusion(bf16[1024,3072]{1,0:T(8,128)(2,1)} %param.7, bf16[1024,768]{1,0:T(8,128)(2,1)S(1)} %copy-done.6), kind=kOutput, calls=%fused_computation.9 | convolution fusion | flops 2417098752 | bytes 9437184 | tf_op jit(solution)/shard_map/dot_general | solution.py:19
  74.8 5.4 %reduce_sum.135 = bf16[16,96,768]{2,1,0:T(8,128)(2,1)} reduce(bf16[16,2,96,768]{3,2,0,1:T(8,128)(2,1)} %all-to-all-done, bf16[]{:T(256)} %constant.44.clone.1), dimensions={1}, to_apply=%region_0.0 | reduce | flops 1179648 | bytes 7077890 | tf_op jit(solution)/shard_map/reduce_sum | solution.py:51
  80.2 8.9 %all_to_all.57 = bf16[16,2,96,384]{3,2,0,1:T(8,128)(2,1)} all-to-all(bf16[16,2,96,384]{3,2,0,1:T(8,128)(2,1)} %copy.27), channel_id=1, replica_groups=mesh['pairs'=16,'core'=2,'fac'=4] {'core'}, dimensions={1} | all-to-all | bytes 4718592 | tf_op jit(solution)/shard_map/all_to_all | solution.py:50
  89.1 7.5 %all-to-all-start.1 = ((bf16[16,96,768]{2,1,0:T(8,128)(2,1)}), bf16[16,96,768]{2,1,0:T(8,128)(2,1)}, u32[]{:S(2)}, u32[]{:S(2)}) async-start(bf16[16,96,768]{2,1,0:T(8,128)(2,1)} %reduce_sum.135), calls=%async_computation.1 | async-start | bytes 4718592 | tf_op jit(solution)/shard_map/all_to_all | solution.py:52
  100.0 32.7 %all-to-all-done.1 = bf16[16,96,768]{2,1,0:T(8,128)(2,1)} async-done(((bf16[16,96,768]{2,1,0:T(8,128)(2,1)}), bf16[16,96,768]{2,1,0:T(8,128)(2,1)}, u32[]{:S(2)}, u32[]{:S(2)}) %all-to-all-start.1) | async-done | bytes 2359328 | tf_op jit(solution)/shard_map/all_to_all | solution.py:52
  139.1 14.8 %all-to-all-done.4 = bf16[16,96,384]{2,1,0:T(8,128)(2,1)} async-done(((bf16[16,96,384]{2,1,0:T(8,128)(2,1)}), bf16[16,96,384]{2,1,0:T(8,128)(2,1)}, u32[]{:S(2)}, u32[]{:S(2)}) %all-to-all-start.4) | async-done | bytes 1179680 | tf_op jit(solution)/shard_map/all_to_all | solution.py:52
  156.7 7.7 %all-to-all-start.2 = ((bf16[32,96,768]{2,1,0:T(8,128)(2,1)}), bf16[32,96,768]{2,1,0:T(8,128)(2,1)}, u32[]{:S(2)}, u32[]{:S(2)}) async-start(bf16[32,96,768]{2,1,0:T(8,128)(2,1)} %stack.22), calls=%async_computation.2 | async-start | bytes 9437184 | tf_op jit(solution)/shard_map/all_to_all | solution.py:10
  166.2 54.0 %all-to-all-done.2 = bf16[32,96,768]{2,1,0:T(8,128)(2,1)} async-done(((bf16[32,96,768]{2,1,0:T(8,128)(2,1)}), bf16[32,96,768]{2,1,0:T(8,128)(2,1)}, u32[]{:S(2)}, u32[]{:S(2)}) %all-to-all-start.2) | async-done | bytes 4718624 | tf_op jit(solution)/shard_map/all_to_all | solution.py:10
  220.2 6.0 %all-to-all-start.6 = ((bf16[16,96,384]{2,1,0:T(8,128)(2,1)}), bf16[16,96,384]{2,1,0:T(8,128)(2,1)S(1)}, u32[]{:S(2)}, u32[]{:S(2)}) async-start(bf16[16,96,384]{2,1,0:T(8,128)(2,1)} %reduce_sum.140), calls=%async_computation.6 | async-start | bytes 2359296 | tf_op jit(solution)/shard_map/all_to_all | solution.py:52
  230.8 11.6 %all_gather.13 = bf16[96,3072]{1,0:T(8,128)(2,1)S(1)} all-gather(bf16[96,768]{1,0:T(8,128)(2,1)S(1)} %fusion.13), channel_id=1, replica_groups=mesh['pairs'=16,'core'=2,'fac'=4] {'fac'}, dimensions={1}, use_global_device_ids=true | all-gather | bytes 737280 | tf_op jit(solution)/shard_map/all_gather | solution.py:82
  248.4 11.7 %all-to-all-start.7 = ((bf16[32,96,768]{2,1,0:T(8,128)(2,1)}), bf16[32,96,768]{2,1,0:T(8,128)(2,1)}, u32[]{:S(2)}, u32[]{:S(2)}) async-start(bf16[32,96,768]{2,1,0:T(8,128)(2,1)} %stack.24), calls=%async_computation.7 | async-start | bytes 9437184 | tf_op jit(solution)/shard_map/all_to_all | solution.py:10
  260.2 11.3 %all_gather.14 = bf16[96,3072]{1,0:T(8,128)(2,1)S(1)} all-gather(bf16[96,768]{1,0:T(8,128)(2,1)S(1)} %pad_maximum_fusion), channel_id=1, replica_groups=mesh['pairs'=16,'core'=2,'fac'=4] {'fac'}, dimensions={1}, use_global_device_ids=true | all-gather | bytes 737280 | tf_op jit(solution)/shard_map/all_gather | solution.py:113
  271.5 44.3 %all-to-all-done.7 = bf16[32,96,768]{2,1,0:T(8,128)(2,1)} async-done(((bf16[32,96,768]{2,1,0:T(8,128)(2,1)}), bf16[32,96,768]{2,1,0:T(8,128)(2,1)}, u32[]{:S(2)}, u32[]{:S(2)}) %all-to-all-start.7) | async-done | bytes 4718624 | tf_op jit(solution)/shard_map/all_to_all | solution.py:10
  321.8 16.9 %all_to_all.58 = f32[128,1,2]{2,1,0:T(1,128)S(1)} all-to-all(f32[128,1,2]{2,1,0:T(1,128)S(1)} %broadcast_in_dim.7), channel_id=1, replica_groups=mesh['pairs'=16,'core'=2,'fac'=4] {'pairs','core','fac'}, dimensions={0} | all-to-all | bytes 2048 | tf_op jit(solution)/shard_map/all_to_all | solution.py:59
  341.3 5.1 %all-to-all-start.9 = ((bf16[32,96,768]{2,1,0:T(8,128)(2,1)}), bf16[32,96,768]{2,1,0:T(8,128)(2,1)}, u32[]{:S(2)}, u32[]{:S(2)}) async-start(bf16[32,96,768]{2,1,0:T(8,128)(2,1)} %stack.27), calls=%async_computation.9 | async-start | bytes 9437184 | tf_op jit(solution)/shard_map/all_to_all | solution.py:10
  349.7 11.9 %all_gather.15 = bf16[96,3072]{1,0:T(8,128)(2,1)} all-gather(bf16[96,768]{1,0:T(8,128)(2,1)S(1)} %convolution_convert_fusion.4), channel_id=1, replica_groups=mesh['pairs'=16,'core'=2,'fac'=4] {'fac'}, dimensions={1}, use_global_device_ids=true | all-gather | bytes 737280 | tf_op jit(solution)/shard_map/all_gather | solution.py:122
  363.7 38.6 %all-to-all-done.9 = bf16[32,96,768]{2,1,0:T(8,128)(2,1)} async-done(((bf16[32,96,768]{2,1,0:T(8,128)(2,1)}), bf16[32,96,768]{2,1,0:T(8,128)(2,1)}, u32[]{:S(2)}, u32[]{:S(2)}) %all-to-all-start.9) | async-done | bytes 4718624 | tf_op jit(solution)/shard_map/all_to_all | solution.py:10
  405.8 7.0 %fusion = bf16[3072,768]{1,0:T(8,128)(2,1)} fusion(f32[32,96,768]{2,1,0:T(8,128)S(1)} %convert_multiply_fusion, bf16[3072,768]{1,0:T(8,128)(2,1)} %bitcast.2), kind=kLoop, calls=%fused_computation.2 | loop fusion | flops 7077888 | bytes 18874368 | tf_op jit(solution)/shard_map/convert_element_type | solution.py:128
  436.6 20.8 %all_to_all.59 = f32[128,1,4]{2,1,0:T(1,128)S(1)} all-to-all(f32[128,1,4]{2,1,0:T(1,128)S(1)} %broadcast_in_dim.8), channel_id=1, replica_groups=mesh['pairs'=16,'core'=2,'fac'=4] {'pairs','core','fac'}, dimensions={0} | all-to-all | bytes 4096 | tf_op jit(solution)/shard_map/all_to_all | solution.py:59
  (74 shorter events, 90.9 us)
Async XLA Ops:
  7.2 30.7 %copy-start = (f32[32768]{0:T(1024)S(1)}, f32[32768]{0:T(1024)}, u32[]{:S(2)}) copy-start(f32[32768]{0:T(1024)} %param.11) | copy-start | bytes 393220
  7.2 131.9 %all-gather.2.cloned.1.call-start = ((), (), s32[]{:S(2)}) async-start(), calls=%async_computation.11 | async-start | bytes 4866048 | tf_op jit(solution)/shard_map/all_gather | solution.py:91
  30.5 7.4 %copy-start.9 = (s32[1024]{0:T(1024)S(1)}, s32[1024]{0:T(1024)}, u32[]{:S(2)}) copy-start(s32[1024]{0:T(1024)} %param.9) | copy-start | bytes 12292
  30.5 13.5 %copy-start.8 = (s32[1024]{0:T(1024)S(1)}, s32[1024]{0:T(1024)}, u32[]{:S(2)}) copy-start(s32[1024]{0:T(1024)} %param.10) | copy-start | bytes 12292
  30.5 40.1 %all-to-all-start = ((bf16[16,2,96,768]{3,2,0,1:T(8,128)(2,1)}), bf16[16,2,96,768]{3,2,0,1:T(8,128)(2,1)}, u32[]{:S(2)}, u32[]{:S(2)}) async-start(bf16[16,2,96,768]{3,2,0,1:T(8,128)(2,1)} %copy.25), calls=%async_computation | async-start | bytes 9437184 | tf_op jit(solution)/shard_map/all_to_all | solution.py:50
  45.9 1.1 copy-start.5
  57.0 2.1 copy-start.6
  70.6 9.6 %all-to-all-start.5 = ((bf16[16,2,96,384]{3,2,0,1:T(8,128)(2,1)}), bf16[16,2,96,384]{3,2,0,1:T(8,128)(2,1)S(1)}, u32[]{:S(2)}, u32[]{:S(2)}) async-start(bf16[16,2,96,384]{3,2,0,1:T(8,128)(2,1)} %copy.29), calls=%async_computation.5 | async-start | bytes 4718592 | tf_op jit(solution)/shard_map/all_to_all | solution.py:50
  89.1 43.6 %all-to-all-start.1 = ((bf16[16,96,768]{2,1,0:T(8,128)(2,1)}), bf16[16,96,768]{2,1,0:T(8,128)(2,1)}, u32[]{:S(2)}, u32[]{:S(2)}) async-start(bf16[16,96,768]{2,1,0:T(8,128)(2,1)} %reduce_sum.135), calls=%async_computation.1 | async-start | bytes 4718592 | tf_op jit(solution)/shard_map/all_to_all | solution.py:52
  132.7 21.3 %all-to-all-start.4 = ((bf16[16,96,384]{2,1,0:T(8,128)(2,1)}), bf16[16,96,384]{2,1,0:T(8,128)(2,1)}, u32[]{:S(2)}, u32[]{:S(2)}) async-start(bf16[16,96,384]{2,1,0:T(8,128)(2,1)} %reduce_sum.137), calls=%async_computation.4 | async-start | bytes 2359296 | tf_op jit(solution)/shard_map/all_to_all | solution.py:52
  156.7 63.5 %all-to-all-start.2 = ((bf16[32,96,768]{2,1,0:T(8,128)(2,1)}), bf16[32,96,768]{2,1,0:T(8,128)(2,1)}, u32[]{:S(2)}, u32[]{:S(2)}) async-start(bf16[32,96,768]{2,1,0:T(8,128)(2,1)} %stack.22), calls=%async_computation.2 | async-start | bytes 9437184 | tf_op jit(solution)/shard_map/all_to_all | solution.py:10
  164.4 63.2 %copy-start.7 = (bf16[96,3072]{1,0:T(8,128)(2,1)S(1)}, bf16[96,3072]{1,0:T(8,128)(2,1)}, u32[]{:S(2)}) copy-start(bf16[96,3072]{1,0:T(8,128)(2,1)} %param.12) | copy-start | bytes 1769476
  220.2 25.5 %all-to-all-start.6 = ((bf16[16,96,384]{2,1,0:T(8,128)(2,1)}), bf16[16,96,384]{2,1,0:T(8,128)(2,1)S(1)}, u32[]{:S(2)}, u32[]{:S(2)}) async-start(bf16[16,96,384]{2,1,0:T(8,128)(2,1)} %reduce_sum.140), calls=%async_computation.6 | async-start | bytes 2359296 | tf_op jit(solution)/shard_map/all_to_all | solution.py:52
  245.7 70.1 %copy-start.2 = (f32[96,768]{1,0:T(8,128)}, f32[96,768]{1,0:T(8,128)S(1)}, u32[]{:S(2)}) copy-start(f32[96,768]{1,0:T(8,128)S(1)} %get-tuple-element.26) | copy-start | bytes 884740
  248.4 67.5 %all-to-all-start.7 = ((bf16[32,96,768]{2,1,0:T(8,128)(2,1)}), bf16[32,96,768]{2,1,0:T(8,128)(2,1)}, u32[]{:S(2)}, u32[]{:S(2)}) async-start(bf16[32,96,768]{2,1,0:T(8,128)(2,1)} %stack.24), calls=%async_computation.7 | async-start | bytes 9437184 | tf_op jit(solution)/shard_map/all_to_all | solution.py:10
  341.3 61.0 %all-to-all-start.9 = ((bf16[32,96,768]{2,1,0:T(8,128)(2,1)}), bf16[32,96,768]{2,1,0:T(8,128)(2,1)}, u32[]{:S(2)}, u32[]{:S(2)}) async-start(bf16[32,96,768]{2,1,0:T(8,128)(2,1)} %stack.27), calls=%async_computation.9 | async-start | bytes 9437184 | tf_op jit(solution)/shard_map/all_to_all | solution.py:10
  416.6 6.9 %collective-permute-start = (bf16[192,768]{1,0:T(8,128)(2,1)S(1)}, bf16[192,768]{1,0:T(8,128)(2,1)S(1)}, u32[]{:S(2)}, u32[]{:S(2)}) collective-permute-start(bf16[192,768]{1,0:T(8,128)(2,1)S(1)} %convolution_convert_fusion.2), channel_id=1, source_target_pairs={{0,1},{1,2},{2,3},{3,0},{4,5},{5,6},{6,7},{7,4},{8,9},{9,10},{10,1... | collective-permute-start | bytes 884744 | tf_op jit(solution)/shard_map/ppermute | solution.py:39
  417.0 16.1 %copy-start.3 = (f32[96,768]{1,0:T(8,128)S(1)}, f32[96,768]{1,0:T(8,128)}, u32[]{:S(2)}) copy-start(f32[96,768]{1,0:T(8,128)} %copy-done.2) | copy-start | bytes 884740
  417.0 16.1 %copy-start.4 = (f32[96,768]{1,0:T(8,128)S(1)}, f32[96,768]{1,0:T(8,128)}, u32[]{:S(2)}) copy-start(f32[96,768]{1,0:T(8,128)} %get-tuple-element.27) | copy-start | bytes 884740
  417.0 8.2 %collective-permute-start.1 = (bf16[192,768]{1,0:T(8,128)(2,1)S(1)}, bf16[192,768]{1,0:T(8,128)(2,1)S(1)}, u32[]{:S(2)}, u32[]{:S(2)}) collective-permute-start(bf16[192,768]{1,0:T(8,128)(2,1)S(1)} %convolution_convert_fusion.2), channel_id=1, source_target_pairs={{0,3},{1,0},{2,1},{3,2},{4,7},{5,4},{6,5},{7,6},{8,11},{9,8},{10,9... | collective-permute-start | bytes 884744 | tf_op jit(solution)/shard_map/ppermute | solution.py:42
  423.5 7.9 %collective-permute-start.2 = (bf16[192,768]{1,0:T(8,128)(2,1)S(1)}, bf16[192,768]{1,0:T(8,128)(2,1)S(1)}, u32[]{:S(2)}, u32[]{:S(2)}) collective-permute-start(bf16[192,768]{1,0:T(8,128)(2,1)S(1)} %collective-permute-done), channel_id=1, source_target_pairs={{0,1},{1,2},{2,3},{3,0},{4,5},{5,6},{6,7},{7,4},{8,9},{9,10},{10,1... | collective-permute-start | bytes 884744 | tf_op jit(solution)/shard_map/ppermute | solution.py:39
  423.5 40.1 %copy-start.1 = (f32[32768]{0:T(1024)S(1)}, f32[32768]{0:T(1024)}, u32[]{:S(2)}) copy-start(f32[32768]{0:T(1024)} %param.11) | copy-start | bytes 393220
Sparse Core Ops, SparseCore 0:
  10.8 50.6 all-gather.1
